TPU v7x, 128 devices: a whole 4x4x4 slice. The times are simulated.
128 devices in a mesh: chan: 32 (over x, y_lo, z), blk: 4 (over y_hi, core).
Axes of the slice: x: 4, y: 4 (y_hi: 2, y_lo: 2; y = y_hi * 2 + y_lo), z: 4, core: 2. Of those that a mesh axis runs over, the one named last changes fastest.
Arguments:
- voltages: int32 [2048, 134656], P(('chan', 'blk')), may hold values from -128 to 127
- flags: int32 [2048], P(('chan', 'blk')), may hold values 0 or 1
- model_amp: float32 [128, 2048], P('chan'), may hold values from 0.04 to 0.4
- model_phase: float32 [128, 2048], P('chan'), may hold values from -3.140625 to 3.140625
Outputs:
- visibility: bfloat16 [2, 128, 2048, 2048], P(None, 'chan', 'blk')
- gains: float32 [2, 128, 2048], P(None, None, ('chan', 'blk'))
All inputs are finite; a program needn't handle non-finite values. No bound on the sum of `flags` on one device may be relied on, other than what follows from the above.
Results may differ from a plain program's by a relative error of at most 0.0091.
Values may be sent and summed in bfloat16 or wider, within the bound.
No kernel may reach another device: no remote copies, remote signals or barrier semaphores. Data moves between devices by JAX's collectives and lax.ppermute only.
A program may use at most 256 MiB of HBM per device.

v0:
```python
import math
import jax
import jax.numpy as jnp
from jax import lax
from jax.sharding import PartitionSpec as P

CHANS = 128
FRAME = 512
TAPS = 8
BAND_START = 64
SPECTRA = 256
ITERS = 10


def window_table():
    index = jnp.arange(TAPS * FRAME, dtype=jnp.float32)
    offset = (index - TAPS * FRAME / 2 + 0.5) / FRAME
    taper = 0.5 - 0.5 * jnp.cos(2.0 * math.pi * (index + 0.5) / (TAPS * FRAME))
    return (jnp.sinc(offset) * taper).reshape(TAPS, FRAME)


def transform_table():
    sample = jnp.arange(FRAME, dtype=jnp.int32)
    channel = BAND_START + jnp.arange(CHANS, dtype=jnp.int32)
    angle = (sample[:, None] * channel[None, :] % FRAME).astype(jnp.float32) * (
        2.0 * math.pi / FRAME
    )
    return jnp.stack([jnp.cos(angle), -jnp.sin(angle)], axis=1).astype(jnp.bfloat16)


def channelize(voltages, keep):
    window = window_table()
    table = transform_table()
    count = voltages.shape[0]
    samples = voltages.astype(jnp.float32).reshape(count, SPECTRA + TAPS - 1, FRAME)
    frames = window[0] * samples[:, 0:SPECTRA, :]
    for tap in range(1, TAPS):
        frames = frames + window[tap] * samples[:, tap : tap + SPECTRA, :]
    frames = frames.astype(jnp.bfloat16)
    spectra = jnp.einsum("itj,jrc->cirt", frames, table, preferred_element_type=jnp.float32)
    scale = 1.0 / (64.0 * math.sqrt(FRAME))
    return (spectra * (scale * keep)[None, :, None, None]).astype(jnp.bfloat16)


def update_gains(model_re, model_im, power, product_re, product_im):
    denominator = (model_re * model_re + model_im * model_im) * (power[:, None] + 1e-06)
    new_re = (model_re * product_re + model_im * product_im) / denominator
    new_im = (model_re * product_im - model_im * product_re) / denominator
    return (new_re, new_im)


def shards(voltages, flags, model_amp, model_phase):
    keep = (1 - flags).astype(jnp.float32)
    input_count = voltages.shape[0]
    spectra = channelize(voltages, keep)
    blk_count = lax.axis_size("blk")
    block_index = lax.axis_index("blk")
    grouped = lax.all_gather(spectra, "blk", axis=1, tiled=True)
    turned = lax.all_to_all(grouped, "chan", split_axis=0, concat_axis=1, tiled=True)
    local_chans = turned.shape[0]
    all_inputs = turned.shape[1]
    row_count = all_inputs // blk_count
    whole = turned.reshape(local_chans, all_inputs, 2 * SPECTRA)
    rows = lax.dynamic_slice_in_dim(whole, block_index * row_count, row_count, 1)
    rotated = jnp.concatenate([rows[:, :, SPECTRA:], -rows[:, :, :SPECTRA]], axis=2)
    stacked = jnp.stack([rows, rotated])
    correlation = (
        jnp.einsum("rcpk,cqk->rcpq", stacked, whole, preferred_element_type=jnp.float32) / SPECTRA
    )
    visibility = correlation.astype(jnp.bfloat16)
    high = lax.Precision.HIGHEST
    full_re = model_amp * jnp.cos(model_phase)
    full_im = model_amp * jnp.sin(model_phase)
    model_re = lax.dynamic_slice_in_dim(full_re, block_index * row_count, row_count, 1)
    model_im = lax.dynamic_slice_in_dim(full_im, block_index * row_count, row_count, 1)

    def sweep(gain_re, gain_im):
        probe_re = gain_re * model_re - gain_im * model_im
        probe_im = gain_re * model_im + gain_im * model_re
        probes = lax.all_gather(jnp.stack([probe_re, probe_im]), "blk", axis=2, tiled=True)
        power = jnp.sum(probes * probes, axis=(0, 2))
        products = jnp.einsum("rcpq,scq->rscp", correlation, probes, precision=high)
        product_re = products[0, 0] - products[1, 1]
        product_im = products[0, 1] + products[1, 0]
        return update_gains(model_re, model_im, power, product_re, product_im)

    def paired(step_index, carried):
        first_re, first_im = sweep(carried[0], carried[1])
        second_re, second_im = sweep(first_re, first_im)
        return (0.5 * (second_re + first_re), 0.5 * (second_im + first_im))

    start_re = jnp.ones((local_chans, row_count), jnp.float32)
    start_im = jnp.zeros((local_chans, row_count), jnp.float32)
    gain_re, gain_im = lax.fori_loop(0, ITERS // 2, paired, (start_re, start_im))
    solved = lax.all_gather(jnp.stack([gain_re, gain_im]), "blk", axis=2, tiled=True)
    owners = lax.all_to_all(solved, "chan", split_axis=2, concat_axis=1, tiled=True)
    gains = lax.dynamic_slice_in_dim(owners, block_index * input_count, input_count, 2)
    return (visibility, gains)


def solution(mesh):
    return jax.shard_map(
        shards,
        mesh=mesh,
        in_specs=(P(("chan", "blk"), None), P(("chan", "blk")), P("chan", None), P("chan", None)),
        out_specs=(P(None, "chan", "blk", None), P(None, None, ("chan", "blk"))),
        check_vma=False,
    )
```

profile of v0, /device:TPU:1, one launch (start us, length us, event | category | flops | bytes accessed | tf_op | source)
XLA Modules:
  0.0 805.5 jit_solution(235510974840824915)
XLA Ops:
  7.2 0.1 fusion.49
  7.3 1.2 cosine_convert_fusion
  8.6 5.9 convert_element_type.41
  14.5 10.1 %reshape.358 = f32[16,263,512]{2,1,0:T(8,128)} reshape(f32[16,134656]{1,0:T(8,128)} %convert_element_type.41) | data formatting | bytes 17235968 | tf_op jit(solution)/shard_map/reshape | solution.py:35
  24.6 27.3 %fusion.34 = bf16[128,16,2,256]{3,0,1,2:T(8,128)(2,1)} fusion(f32[16]{0:T(128)S(1)} %convert_multiply_fusion, f32[16,263,512]{2,1,0:T(8,128)} %reshape.358, f32[512]{0:T(512)S(1)} %get-tuple-element.223, f32[512]{0:T(512)S(1)} %get-tuple-element.224, f32[512]{0:T(512)S(1)} %get-tuple-element.225, f32[512]{0:T(512)S(1)} %get-tuple-element.226, ...), kind=kOutput, calls=%fused_computation.70 | convolution fusion | flops 1109917696 | bytes 69484608 | tf_op jit(solution)/shard_map/itj,jrc->cirt/dot_general | solution.py:40
  52.0 66.1 %all-gather.2.cloned.1.call-done = bf16[128,64,2,256]{3,0,1,2:T(8,128)(2,1)} async-done(((bf16[128,16,2,256]{3,0,1,2:T(8,128)(2,1)}), bf16[128,64,2,256]{3,0,1,2:T(8,128)(2,1)}) %all-gather.2.cloned.1.call-update) | async-done | bytes 8388624 | tf_op jit(solution)/shard_map/all_gather | solution.py:58
  118.1 11.5 %copy.43 = bf16[128,64,2,256]{3,1,2,0:T(8,128)(2,1)} copy(bf16[128,64,2,256]{3,0,1,2:T(8,128)(2,1)} %all-gather.2.cloned.1.call-done) | data formatting | bytes 16777216 | tf_op jit(solution)/shard_map/all_gather | solution.py:58
  129.7 7.3 all-to-all-start
  137.0 0.8 multiply_add_fusion.2
  137.8 117.2 %all-to-all-done = bf16[128,64,2,256]{3,1,2,0:T(8,128)(2,1)} async-done(((bf16[128,64,2,256]{3,1,2,0:T(8,128)(2,1)}), bf16[128,64,2,256]{3,1,2,0:T(8,128)(2,1)}, u32[]{:S(2)}, u32[]{:S(2)}) %all-to-all-start) | async-done | bytes 8388640 | tf_op jit(solution)/shard_map/all_to_all | solution.py:59
  254.9 16.4 %copy.81 = bf16[32,4,64,2,256]{4,3,2,0,1:T(2,128)(2,1)} copy(bf16[32,4,64,2,256]{4,2,3,1,0:T(8,128)(2,1)} %bitcast.4) | data formatting | bytes 16777216 | tf_op jit(solution)/shard_map/all_to_all | solution.py:59
  271.4 14.1 %reshape.359 = bf16[4,2048,512]{2,1,0:T(8,128)(2,1)} reshape(bf16[4,32,64,2,256]{4,3,2,1,0:T(2,128)(2,1)} %bitcast.199) | data formatting | bytes 16777216 | tf_op jit(solution)/shard_map/reshape | solution.py:63
  285.4 14.1 %reshape.366 = bf16[4,2048,512,1]{2,1,0,3:T(8,128)(2,1)} reshape(bf16[4,32,64,2,256]{4,3,2,1,0:T(2,128)(2,1)} %bitcast.200) | data formatting | bytes 16777216 | tf_op jit(solution)/shard_map/reshape | solution.py:63
  299.5 1.8 constant_dynamic-slice_fusion
  301.3 3.3 maximum_bitcast_fusion
  304.6 22.1 %fusion.78 = (bf16[2,4,512,2048]{2,3,0,1:T(8,128)(2,1)}, f32[2,4,512,2048]{2,3,0,1:T(8,128)}) fusion(bf16[1,4,512,512]{3,2,0,1:T(8,128)(2,1)S(1)} %get-tuple-element.234, bf16[1,4,512,512]{3,2,0,1:T(8,128)(2,1)} %get-tuple-element.235, bf16[4,2048,512,1]{2,1,0,3:T(8,128)(2,1)} %reshape.366), kind=kOutput, calls=%fused_computation.137 | convolution fusion | flops 8615100416 | bytes 62914560 | tf_op jit(solution)/shard_map/rcpk,cqk->rcpq/dot_general | solution.py:68
  326.7 31.8 %copy.45 = f32[2,4,512,2048]{3,2,0,1:T(8,128)} copy(f32[2,4,512,2048]{2,3,0,1:T(8,128)} %get-tuple-element.233) | data formatting | bytes 67108864
  358.5 381.5 %while.16 = (s32[]{:T(128)}, f32[4,512]{1,0:T(4,128)S(1)}, f32[4,512]{1,0:T(4,128)S(1)}, f32[4,512]{1,0:T(4,128)S(1)}, f32[4,512]{1,0:T(4,128)S(1)}, /*index=5*/...) while((s32[]{:T(128)}, f32[4,512]{1,0:T(4,128)S(1)}, ...), condition=%wide.region_3.4_spmd.clone, body=%wide.region_0.3_spmd.clone.sunk | while | flops 402845696 | bytes 68075792 | solution.py:94
  358.6 8.9 %all_gather.24 = f32[2,4,2048]{2,0,1:T(2,128)S(1)} all-gather(f32[2,4,512]{2,0,1:T(2,128)S(1)} %pad_maximum_fusion.5), channel_id=1, replica_groups=mesh['chan'=32,'blk'=4] {'blk'}, dimensions={2}, use_global_device_ids=true | all-gather | bytes 81920 | tf_op jit(solution)/shard_map/while/body/eval_jaxpr/all_gather | solution.py:80
  367.5 30.8 %convolution_bitcast_fusion.2 = f32[2,2,4,512]{3,1,0,2:T(2,128)S(1)} fusion(f32[2,4,512,2048]{3,2,0,1:T(8,128)} %get-tuple-element.328, f32[2,4,2048]{2,0,1:T(2,128)S(1)} %all_gather.24), kind=kOutput, calls=%fused_computation.clone.1 | convolution fusion | flops 201326592 | bytes 33652736 | tf_op jit(solution)/shard_map/while/body/eval_jaxpr/rcpq,scq->rscp/dot_general | solution.py:82
  398.3 0.1 multiply_reduce_fusion.4
  398.6 6.8 all_gather.25
  405.4 30.8 %fusion.97 = f32[4,2,2,512]{3,1,2,0:T(2,128)S(1)} fusion(f32[2,4,512,2048]{3,2,0,1:T(8,128)} %get-tuple-element.328, f32[2,4,2048,1]{2,1,0,3:T(4,128)S(1)} %bitcast.201), kind=kOutput, calls=%fused_computation.2.clone.1 | convolution fusion | flops 201326592 | bytes 33652736 | tf_op jit(solution)/shard_map/while/body/eval_jaxpr/rcpq,scq->rscp/dot_general | solution.py:82
  436.2 0.1 multiply_reduce_fusion.5
  436.4 0.1 fusion.98
  436.6 6.8 all_gather.24
  443.3 30.8 %convolution_bitcast_fusion.2 = f32[2,2,4,512]{3,1,0,2:T(2,128)S(1)} fusion(f32[2,4,512,2048]{3,2,0,1:T(8,128)} %get-tuple-element.328, f32[2,4,2048]{2,0,1:T(2,128)S(1)} %all_gather.24), kind=kOutput, calls=%fused_computation.clone.1 | convolution fusion | flops 201326592 | bytes 33652736 | tf_op jit(solution)/shard_map/while/body/eval_jaxpr/rcpq,scq->rscp/dot_general | solution.py:82
  474.1 0.1 multiply_reduce_fusion.4
  474.5 6.8 all_gather.25
  481.2 30.8 %fusion.97 = f32[4,2,2,512]{3,1,2,0:T(2,128)S(1)} fusion(f32[2,4,512,2048]{3,2,0,1:T(8,128)} %get-tuple-element.328, f32[2,4,2048,1]{2,1,0,3:T(4,128)S(1)} %bitcast.201), kind=kOutput, calls=%fused_computation.2.clone.1 | convolution fusion | flops 201326592 | bytes 33652736 | tf_op jit(solution)/shard_map/while/body/eval_jaxpr/rcpq,scq->rscp/dot_general | solution.py:82
  512.1 0.1 multiply_reduce_fusion.5
  512.2 0.1 fusion.98
  512.4 6.8 all_gather.24
  519.2 30.8 %convolution_bitcast_fusion.2 = f32[2,2,4,512]{3,1,0,2:T(2,128)S(1)} fusion(f32[2,4,512,2048]{3,2,0,1:T(8,128)} %get-tuple-element.328, f32[2,4,2048]{2,0,1:T(2,128)S(1)} %all_gather.24), kind=kOutput, calls=%fused_computation.clone.1 | convolution fusion | flops 201326592 | bytes 33652736 | tf_op jit(solution)/shard_map/while/body/eval_jaxpr/rcpq,scq->rscp/dot_general | solution.py:82
  550.0 0.1 multiply_reduce_fusion.4
  550.3 6.8 all_gather.25
  557.0 30.8 %fusion.97 = f32[4,2,2,512]{3,1,2,0:T(2,128)S(1)} fusion(f32[2,4,512,2048]{3,2,0,1:T(8,128)} %get-tuple-element.328, f32[2,4,2048,1]{2,1,0,3:T(4,128)S(1)} %bitcast.201), kind=kOutput, calls=%fused_computation.2.clone.1 | convolution fusion | flops 201326592 | bytes 33652736 | tf_op jit(solution)/shard_map/while/body/eval_jaxpr/rcpq,scq->rscp/dot_general | solution.py:82
  587.9 0.1 multiply_reduce_fusion.5
  588.0 0.1 fusion.98
  588.2 6.8 all_gather.24
  595.0 30.8 %convolution_bitcast_fusion.2 = f32[2,2,4,512]{3,1,0,2:T(2,128)S(1)} fusion(f32[2,4,512,2048]{3,2,0,1:T(8,128)} %get-tuple-element.328, f32[2,4,2048]{2,0,1:T(2,128)S(1)} %all_gather.24), kind=kOutput, calls=%fused_computation.clone.1 | convolution fusion | flops 201326592 | bytes 33652736 | tf_op jit(solution)/shard_map/while/body/eval_jaxpr/rcpq,scq->rscp/dot_general | solution.py:82
  625.8 0.1 multiply_reduce_fusion.4
  626.1 6.8 all_gather.25
  632.9 30.8 %fusion.97 = f32[4,2,2,512]{3,1,2,0:T(2,128)S(1)} fusion(f32[2,4,512,2048]{3,2,0,1:T(8,128)} %get-tuple-element.328, f32[2,4,2048,1]{2,1,0,3:T(4,128)S(1)} %bitcast.201), kind=kOutput, calls=%fused_computation.2.clone.1 | convolution fusion | flops 201326592 | bytes 33652736 | tf_op jit(solution)/shard_map/while/body/eval_jaxpr/rcpq,scq->rscp/dot_general | solution.py:82
  663.7 0.1 multiply_reduce_fusion.5
  663.9 0.1 fusion.98
  664.1 6.8 all_gather.24
  670.8 30.8 %convolution_bitcast_fusion.2 = f32[2,2,4,512]{3,1,0,2:T(2,128)S(1)} fusion(f32[2,4,512,2048]{3,2,0,1:T(8,128)} %get-tuple-element.328, f32[2,4,2048]{2,0,1:T(2,128)S(1)} %all_gather.24), kind=kOutput, calls=%fused_computation.clone.1 | convolution fusion | flops 201326592 | bytes 33652736 | tf_op jit(solution)/shard_map/while/body/eval_jaxpr/rcpq,scq->rscp/dot_general | solution.py:82
  701.6 0.1 multiply_reduce_fusion.4
  701.9 6.8 all_gather.25
  708.7 30.8 %fusion.97 = f32[4,2,2,512]{3,1,2,0:T(2,128)S(1)} fusion(f32[2,4,512,2048]{3,2,0,1:T(8,128)} %get-tuple-element.328, f32[2,4,2048,1]{2,1,0,3:T(4,128)S(1)} %bitcast.201), kind=kOutput, calls=%fused_computation.2.clone.1 | convolution fusion | flops 201326592 | bytes 33652736 | tf_op jit(solution)/shard_map/while/body/eval_jaxpr/rcpq,scq->rscp/dot_general | solution.py:82
  739.5 0.1 multiply_reduce_fusion.5
  739.7 0.1 fusion.98
  740.0 6.8 all_gather.19
  746.8 1.1 copy.46
  747.9 3.8 reshape.368
  751.7 18.3 %all-to-all-start.1 = ((f32[32,1,512]{2,1,0:T(1,128)}), f32[32,1,512]{2,1,0:T(1,128)S(1)}, u32[]{:S(2)}, u32[]{:S(2)}) async-start(f32[32,1,512]{2,1,0:T(1,128)} %reshape.368), calls=%async_computation.1 | async-start | bytes 131072 | tf_op jit(solution)/shard_map/all_to_all | solution.py:96
  770.0 21.5 %copy.48 = bf16[2,4,512,2048]{3,2,1,0:T(8,128)(2,1)} copy(bf16[2,4,512,2048]{2,3,0,1:T(8,128)(2,1)} %get-tuple-element.232) | data formatting | bytes 33554432
  791.5 0.5 broadcast.226
  792.0 0.8 reduce
  792.8 3.2 reshape.369
  796.1 1.9 copy.47
  797.9 0.1 constant_dynamic-slice_fusion.1
  798.0 0.7 copy.49
  (66 shorter events, 1.5 us)
Async XLA Ops:
  7.2 111.0 %all-gather.2.cloned.1.call-start = ((), (), s32[]{:S(2)}) async-start(), calls=%async_computation.2 | async-start | bytes 10485760 | tf_op jit(solution)/shard_map/all_gather | solution.py:58
  14.5 10.2 %copy-start = (s32[16]{0:T(128)S(1)}, s32[16]{0:T(128)}, u32[]{:S(2)}) copy-start(s32[16]{0:T(128)} %param.7) | copy-start | bytes 196
  129.7 125.3 %all-to-all-start = ((bf16[128,64,2,256]{3,1,2,0:T(8,128)(2,1)}), bf16[128,64,2,256]{3,1,2,0:T(8,128)(2,1)}, u32[]{:S(2)}, u32[]{:S(2)}) async-start(bf16[128,64,2,256]{3,1,2,0:T(8,128)(2,1)} %copy.43), calls=%async_computation | async-start | bytes 16777216 | tf_op jit(solution)/shard_map/all_to_all | solution.py:59
  751.7 39.8 %all-to-all-start.1 = ((f32[32,1,512]{2,1,0:T(1,128)}), f32[32,1,512]{2,1,0:T(1,128)S(1)}, u32[]{:S(2)}, u32[]{:S(2)}) async-start(f32[32,1,512]{2,1,0:T(1,128)} %reshape.368), calls=%async_computation.1 | async-start | bytes 131072 | tf_op jit(solution)/shard_map/all_to_all | solution.py:96
Sparse Core Ops, SparseCore 0:
  52.1 65.9 all-gather.1
where the time goes:
time: 808 us; the launch traced here: 806 us
  matrix products  357 us (44%)
  waiting for transfers between devices  183 us (23%)
  local copies, waits for them, and re-layouts  131 us (16%)
  blocking collectives  76.4 us (9%)
  starting transfers between devices  25.6 us (3%)
  other arithmetic  17 us (2%)
  between operations  14.2 us (2%)
    dot_general x10, matrix products, sweep(): products = jnp.einsum('rcpq,scq->rscp', correlation, probes, precision=high)  308 us
    all_to_all x1, waiting for transfers between devices, shards(): lax.all_to_all(grouped, 'chan', split_axis=0, concat_axis=1, tiled=True)  117 us
    all_gather x10, blocking collectives, sweep(): lax.all_gather(jnp.stack([probe_re, probe_im]), 'blk', axis=2, tiled=True)  69.7 us
    all_gather x1, waiting for transfers between devices, shards(): grouped = lax.all_gather(spectra, 'blk', axis=1, tiled=True)  66.1 us
    unnamed x7, local copies, waits for them, and re-layouts  61 us
    reshape x2, local copies, waits for them, and re-layouts, shards(): whole = turned.reshape(local_chans, all_inputs, 2 * SPECTRA)  28.1 us
    dot_general x1, matrix products, channelize(): jnp.einsum('itj,jrc->cirt', frames, table, preferred_element_type=jnp.flo...  27.3 us
    dot_general x1, matrix products, shards(): jnp.einsum('rcpk,cqk->rcpq', stacked, whole, preferred_element_type=jnp.f...  22.1 us
  transfers between devices with their start and end apart: 3, of which 2 were waited for; matrix products, arithmetic and copies ran while one was open for 3% of the time, Pallas kernels for 0%

commit v1 on v0

--- a/solution.py
+++ b/solution.py
@@ -77,7 +77,12 @@
     def sweep(gain_re, gain_im):
         probe_re = gain_re * model_re - gain_im * model_im
         probe_im = gain_re * model_im + gain_im * model_re
-        probes = lax.all_gather(jnp.stack([probe_re, probe_im]), "blk", axis=2, tiled=True)
+        probes = jnp.concatenate(
+            lax.all_to_all(
+                jnp.stack([jnp.stack([probe_re, probe_im])] * lax.axis_size("blk")), "blk", 0, 0
+            ),
+            axis=2,
+        )
         power = jnp.sum(probes * probes, axis=(0, 2))
         products = jnp.einsum("rcpq,scq->rscp", correlation, probes, precision=high)
         product_re = products[0, 0] - products[1, 1]

time: 808 us -> 830 us (1.027)
  blocking collectives: 76.4 us -> 49.6 us
  waiting for transfers between devices: 183 us -> 207 us
  starting transfers between devices: 25.6 us -> 45.6 us
    all_gather x10 -> x0, blocking collectives: 69.7 us -> none  [sweep(): lax.all_gather(jnp.stack([probe_re, probe_im]), 'blk', axis=2, tiled=True)]
    all_to_all x0 -> x5, blocking collectives: none -> 42.2 us  [sweep(): lax.all_to_all(jnp.stack([jnp.stack([probe_re, probe_im])] * lax.axis_siz...]
    all_to_all x0 -> x5, waiting for transfers between devices: none -> 23.8 us  [sweep(): lax.all_to_all(jnp.stack([jnp.stack([probe_re, probe_im])] * lax.axis_siz...]
    all_to_all x0 -> x5, starting transfers between devices: none -> 20.6 us  [sweep(): lax.all_to_all(jnp.stack([jnp.stack([probe_re, probe_im])] * lax.axis_siz...]
  transfers between devices with their start and end apart: 3 -> 8, of which waited for: 2 -> 7; matrix products, arithmetic and copies ran while one was open for 3% -> 3% of each run, Pallas kernels for 0% -> 0%
where the time goes in v1:
time: 830 us; the launch traced here: 827 us
  matrix products  357 us (43%)
  waiting for transfers between devices  207 us (25%)
  local copies, waits for them, and re-layouts  136 us (16%)
  blocking collectives  49.6 us (6%)
  starting transfers between devices  45.6 us (5%)
  other arithmetic  16.9 us (2%)
  between operations  14.2 us (2%)
    dot_general x10, matrix products, sweep(): products = jnp.einsum('rcpq,scq->rscp', correlation, probes, precision=high)  308 us
    all_to_all x1, waiting for transfers between devices, shards(): lax.all_to_all(grouped, 'chan', split_axis=0, concat_axis=1, tiled=True)  117 us
    all_gather x1, waiting for transfers between devices, shards(): grouped = lax.all_gather(spectra, 'blk', axis=1, tiled=True)  66.1 us
    unnamed x7, local copies, waits for them, and re-layouts  61.2 us
    all_to_all x5, blocking collectives, sweep(): lax.all_to_all(jnp.stack([jnp.stack([probe_re, probe_im])] * lax.axis_siz...  42.2 us
    reshape x2, local copies, waits for them, and re-layouts, shards(): whole = turned.reshape(local_chans, all_inputs, 2 * SPECTRA)  28.1 us
    dot_general x1, matrix products, channelize(): jnp.einsum('itj,jrc->cirt', frames, table, preferred_element_type=jnp.flo...  27.4 us
    all_to_all x5, waiting for transfers between devices, sweep(): lax.all_to_all(jnp.stack([jnp.stack([probe_re, probe_im])] * lax.axis_siz...  23.8 us
  transfers between devices with their start and end apart: 8, of which 7 were waited for; matrix products, arithmetic and copies ran while one was open for 3% of the time, Pallas kernels for 0%

profile of v1, /device:TPU:1, one launch (start us, length us, event | category | flops | bytes accessed | tf_op | source)
XLA Modules:
  0.0 826.9 jit_solution(1450118675787675744)
XLA Ops:
  7.3 1.2 cosine_convert_fusion
  8.6 5.9 convert_element_type.41
  14.5 10.1 %reshape.386 = f32[16,263,512]{2,1,0:T(8,128)} reshape(f32[16,134656]{1,0:T(8,128)} %convert_element_type.41) | data formatting | bytes 17235968 | tf_op jit(solution)/shard_map/reshape | solution.py:35
  24.7 27.4 %fusion.34 = bf16[128,16,2,256]{3,0,1,2:T(8,128)(2,1)} fusion(f32[16]{0:T(128)S(1)} %convert_multiply_fusion, f32[16,263,512]{2,1,0:T(8,128)} %reshape.386, f32[512]{0:T(512)S(1)} %get-tuple-element.223, f32[512]{0:T(512)S(1)} %get-tuple-element.224, f32[512]{0:T(512)S(1)} %get-tuple-element.225, f32[512]{0:T(512)S(1)} %get-tuple-element.226, ...), kind=kOutput, calls=%fused_computation.70 | convolution fusion | flops 1109917696 | bytes 69484608 | tf_op jit(solution)/shard_map/itj,jrc->cirt/dot_general | solution.py:40
  52.0 66.1 %all-gather.2.cloned.1.call-done = bf16[128,64,2,256]{3,0,1,2:T(8,128)(2,1)} async-done(((bf16[128,16,2,256]{3,0,1,2:T(8,128)(2,1)}), bf16[128,64,2,256]{3,0,1,2:T(8,128)(2,1)}) %all-gather.2.cloned.1.call-update) | async-done | bytes 8388624 | tf_op jit(solution)/shard_map/all_gather | solution.py:58
  118.2 11.5 %copy.47 = bf16[128,64,2,256]{3,1,2,0:T(8,128)(2,1)} copy(bf16[128,64,2,256]{3,0,1,2:T(8,128)(2,1)} %all-gather.2.cloned.1.call-done) | data formatting | bytes 16777216 | tf_op jit(solution)/shard_map/all_gather | solution.py:58
  129.7 7.3 all-to-all-start.2
  137.0 0.8 multiply_add_fusion.1
  137.8 117.2 %all-to-all-done.2 = bf16[128,64,2,256]{3,1,2,0:T(8,128)(2,1)} async-done(((bf16[128,64,2,256]{3,1,2,0:T(8,128)(2,1)}), bf16[128,64,2,256]{3,1,2,0:T(8,128)(2,1)}, u32[]{:S(2)}, u32[]{:S(2)}) %all-to-all-start.2) | async-done | bytes 8388640 | tf_op jit(solution)/shard_map/all_to_all | solution.py:59
  255.0 16.4 %copy.81 = bf16[32,4,64,2,256]{4,3,2,0,1:T(2,128)(2,1)} copy(bf16[32,4,64,2,256]{4,2,3,1,0:T(8,128)(2,1)} %bitcast.4) | data formatting | bytes 16777216 | tf_op jit(solution)/shard_map/all_to_all | solution.py:59
  271.4 14.1 %reshape.387 = bf16[4,2048,512]{2,1,0:T(8,128)(2,1)} reshape(bf16[4,32,64,2,256]{4,3,2,1,0:T(2,128)(2,1)} %bitcast.217) | data formatting | bytes 16777216 | tf_op jit(solution)/shard_map/reshape | solution.py:63
  285.5 14.0 %reshape.398 = bf16[4,2048,512,1]{2,1,0,3:T(8,128)(2,1)} reshape(bf16[4,32,64,2,256]{4,3,2,1,0:T(2,128)(2,1)} %bitcast.218) | data formatting | bytes 16777216 | tf_op jit(solution)/shard_map/reshape | solution.py:63
  299.5 1.8 constant_dynamic-slice_fusion
  301.3 3.3 maximum_bitcast_fusion
  304.7 22.1 %fusion.78 = (bf16[2,4,512,2048]{2,3,0,1:T(8,128)(2,1)}, f32[2,4,512,2048]{2,3,0,1:T(8,128)}) fusion(bf16[1,4,512,512]{3,2,0,1:T(8,128)(2,1)S(1)} %get-tuple-element.234, bf16[1,4,512,512]{3,2,0,1:T(8,128)(2,1)} %get-tuple-element.235, bf16[4,2048,512,1]{2,1,0,3:T(8,128)(2,1)} %reshape.398), kind=kOutput, calls=%fused_computation.137 | convolution fusion | flops 8615100416 | bytes 62914560 | tf_op jit(solution)/shard_map/rcpk,cqk->rcpq/dot_general | solution.py:68
  326.7 32.0 %copy.49 = f32[2,4,512,2048]{3,2,0,1:T(8,128)} copy(f32[2,4,512,2048]{2,3,0,1:T(8,128)} %get-tuple-element.233) | data formatting | bytes 67108864
  358.7 402.6 %while.16 = (s32[]{:T(128)}, f32[4,512]{1,0:T(4,128)S(1)}, f32[4,512]{1,0:T(4,128)S(1)}, f32[4,512]{1,0:T(4,128)S(1)}, f32[4,512]{1,0:T(4,128)S(1)}, /*index=5*/...) while((s32[]{:T(128)}, f32[4,512]{1,0:T(4,128)S(1)}, ...), condition=%wide.region_3.4_spmd.clone, body=%wide.region_0.3_spmd.clone.sunk | while | flops 402845696 | bytes 68960560 | solution.py:99
  358.8 10.2 %all_to_all.53 = f32[4,2,4,512]{3,1,2,0:T(2,128)S(1)} all-to-all(f32[4,2,4,512]{3,1,2,0:T(2,128)S(1)} %stack.79), channel_id=1, replica_groups=mesh['chan'=32,'blk'=4] {'blk'}, dimensions={0} | all-to-all | bytes 131072 | tf_op jit(solution)/shard_map/while/body/eval_jaxpr/all_to_all | solution.py:81
  369.1 30.8 %convolution_bitcast_fusion.2 = f32[2,2,4,512]{3,1,0,2:T(2,128)S(1)} fusion(f32[2,4,512,2048]{3,2,0,1:T(8,128)} %get-tuple-element.328, f32[2,4,2048,1]{2,0,1,3:T(2,128)S(1)} %reshape.406), kind=kOutput, calls=%fused_computation.clone.1 | convolution fusion | flops 201326592 | bytes 33652736 | tf_op jit(solution)/shard_map/while/body/eval_jaxpr/rcpq,scq->rscp/dot_general | solution.py:87
  399.9 0.1 multiply_reduce_fusion.4
  400.2 0.6 stack.80
  400.9 4.1 all-to-all-start.1
  405.0 4.8 all-to-all-done.1
  409.9 30.8 %fusion.97 = f32[4,2,2,512]{3,1,2,0:T(2,128)S(1)} fusion(f32[2,4,512,2048]{3,2,0,1:T(8,128)} %get-tuple-element.328, f32[2,4,2048,1]{2,0,1,3:T(2,128)S(1)} %reshape.407), kind=kOutput, calls=%fused_computation.1.clone.1 | convolution fusion | flops 201326592 | bytes 33652736 | tf_op jit(solution)/shard_map/while/body/eval_jaxpr/rcpq,scq->rscp/dot_general | solution.py:87
  440.7 0.1 multiply_reduce_fusion.5
  441.0 8.0 all_to_all.53
  449.1 30.8 %convolution_bitcast_fusion.2 = f32[2,2,4,512]{3,1,0,2:T(2,128)S(1)} fusion(f32[2,4,512,2048]{3,2,0,1:T(8,128)} %get-tuple-element.328, f32[2,4,2048,1]{2,0,1,3:T(2,128)S(1)} %reshape.406), kind=kOutput, calls=%fused_computation.clone.1 | convolution fusion | flops 201326592 | bytes 33652736 | tf_op jit(solution)/shard_map/while/body/eval_jaxpr/rcpq,scq->rscp/dot_general | solution.py:87
  480.0 0.1 multiply_reduce_fusion.4
  480.3 0.6 stack.80
  480.9 4.1 all-to-all-start.1
  485.1 4.8 all-to-all-done.1
  489.9 30.8 %fusion.97 = f32[4,2,2,512]{3,1,2,0:T(2,128)S(1)} fusion(f32[2,4,512,2048]{3,2,0,1:T(8,128)} %get-tuple-element.328, f32[2,4,2048,1]{2,0,1,3:T(2,128)S(1)} %reshape.407), kind=kOutput, calls=%fused_computation.1.clone.1 | convolution fusion | flops 201326592 | bytes 33652736 | tf_op jit(solution)/shard_map/while/body/eval_jaxpr/rcpq,scq->rscp/dot_general | solution.py:87
  520.7 0.1 multiply_reduce_fusion.5
  521.1 8.0 all_to_all.53
  529.2 30.8 %convolution_bitcast_fusion.2 = f32[2,2,4,512]{3,1,0,2:T(2,128)S(1)} fusion(f32[2,4,512,2048]{3,2,0,1:T(8,128)} %get-tuple-element.328, f32[2,4,2048,1]{2,0,1,3:T(2,128)S(1)} %reshape.406), kind=kOutput, calls=%fused_computation.clone.1 | convolution fusion | flops 201326592 | bytes 33652736 | tf_op jit(solution)/shard_map/while/body/eval_jaxpr/rcpq,scq->rscp/dot_general | solution.py:87
  560.0 0.1 multiply_reduce_fusion.4
  560.3 0.6 stack.80
  561.0 4.1 all-to-all-start.1
  565.1 4.8 all-to-all-done.1
  570.0 30.8 %fusion.97 = f32[4,2,2,512]{3,1,2,0:T(2,128)S(1)} fusion(f32[2,4,512,2048]{3,2,0,1:T(8,128)} %get-tuple-element.328, f32[2,4,2048,1]{2,0,1,3:T(2,128)S(1)} %reshape.407), kind=kOutput, calls=%fused_computation.1.clone.1 | convolution fusion | flops 201326592 | bytes 33652736 | tf_op jit(solution)/shard_map/while/body/eval_jaxpr/rcpq,scq->rscp/dot_general | solution.py:87
  600.8 0.1 multiply_reduce_fusion.5
  601.1 8.0 all_to_all.53
  609.2 30.8 %convolution_bitcast_fusion.2 = f32[2,2,4,512]{3,1,0,2:T(2,128)S(1)} fusion(f32[2,4,512,2048]{3,2,0,1:T(8,128)} %get-tuple-element.328, f32[2,4,2048,1]{2,0,1,3:T(2,128)S(1)} %reshape.406), kind=kOutput, calls=%fused_computation.clone.1 | convolution fusion | flops 201326592 | bytes 33652736 | tf_op jit(solution)/shard_map/while/body/eval_jaxpr/rcpq,scq->rscp/dot_general | solution.py:87
  640.0 0.1 multiply_reduce_fusion.4
  640.4 0.6 stack.80
  641.0 4.1 all-to-all-start.1
  645.1 4.8 all-to-all-done.1
  650.0 30.8 %fusion.97 = f32[4,2,2,512]{3,1,2,0:T(2,128)S(1)} fusion(f32[2,4,512,2048]{3,2,0,1:T(8,128)} %get-tuple-element.328, f32[2,4,2048,1]{2,0,1,3:T(2,128)S(1)} %reshape.407), kind=kOutput, calls=%fused_computation.1.clone.1 | convolution fusion | flops 201326592 | bytes 33652736 | tf_op jit(solution)/shard_map/while/body/eval_jaxpr/rcpq,scq->rscp/dot_general | solution.py:87
  681.2 8.0 all_to_all.53
  689.3 30.8 %convolution_bitcast_fusion.2 = f32[2,2,4,512]{3,1,0,2:T(2,128)S(1)} fusion(f32[2,4,512,2048]{3,2,0,1:T(8,128)} %get-tuple-element.328, f32[2,4,2048,1]{2,0,1,3:T(2,128)S(1)} %reshape.406), kind=kOutput, calls=%fused_computation.clone.1 | convolution fusion | flops 201326592 | bytes 33652736 | tf_op jit(solution)/shard_map/while/body/eval_jaxpr/rcpq,scq->rscp/dot_general | solution.py:87
  720.4 0.6 stack.80
  721.1 4.1 all-to-all-start.1
  725.2 4.8 all-to-all-done.1
  730.1 30.8 %fusion.97 = f32[4,2,2,512]{3,1,2,0:T(2,128)S(1)} fusion(f32[2,4,512,2048]{3,2,0,1:T(8,128)} %get-tuple-element.328, f32[2,4,2048,1]{2,0,1,3:T(2,128)S(1)} %reshape.407), kind=kOutput, calls=%fused_computation.1.clone.1 | convolution fusion | flops 201326592 | bytes 33652736 | tf_op jit(solution)/shard_map/while/body/eval_jaxpr/rcpq,scq->rscp/dot_general | solution.py:87
  761.3 7.4 all_gather.7
  768.8 1.1 copy.50
  769.9 3.8 reshape.402
  773.7 17.7 %all-to-all-start.3 = ((f32[32,1,512]{2,1,0:T(1,128)}), f32[32,1,512]{2,1,0:T(1,128)S(1)}, u32[]{:S(2)}, u32[]{:S(2)}) async-start(f32[32,1,512]{2,1,0:T(1,128)} %reshape.402), calls=%async_computation.3 | async-start | bytes 131072 | tf_op jit(solution)/shard_map/all_to_all | solution.py:101
  791.4 21.5 %copy.52 = bf16[2,4,512,2048]{3,2,1,0:T(8,128)(2,1)} copy(bf16[2,4,512,2048]{2,3,0,1:T(8,128)(2,1)} %get-tuple-element.232) | data formatting | bytes 33554432
  812.9 0.5 broadcast.236
  813.4 0.8 reduce.2
  814.2 3.2 reshape.403
  817.5 1.9 copy.51
  819.4 0.7 copy.53
  (101 shorter events, 3.7 us)
Async XLA Ops:
  7.2 111.0 %all-gather.2.cloned.1.call-start = ((), (), s32[]{:S(2)}) async-start(), calls=%async_computation.4 | async-start | bytes 10485760 | tf_op jit(solution)/shard_map/all_gather | solution.py:58
  14.5 10.2 %copy-start = (s32[16]{0:T(128)S(1)}, s32[16]{0:T(128)}, u32[]{:S(2)}) copy-start(s32[16]{0:T(128)} %param.7) | copy-start | bytes 196
  129.7 125.3 %all-to-all-start.2 = ((bf16[128,64,2,256]{3,1,2,0:T(8,128)(2,1)}), bf16[128,64,2,256]{3,1,2,0:T(8,128)(2,1)}, u32[]{:S(2)}, u32[]{:S(2)}) async-start(bf16[128,64,2,256]{3,1,2,0:T(8,128)(2,1)} %copy.47), calls=%async_computation.2 | async-start | bytes 16777216 | tf_op jit(solution)/shard_map/all_to_all | solution.py:59
  400.9 8.9 %all-to-all-start.1 = ((f32[4,2,4,512]{3,1,2,0:T(2,128)}), f32[4,2,4,512]{3,1,2,0:T(2,128)S(1)}, u32[]{:S(2)}, u32[]{:S(2)}) async-start(f32[4,2,4,512]{3,1,2,0:T(2,128)} %stack.80), calls=%async_computation.1 | async-start | bytes 131072 | tf_op jit(solution)/shard_map/while/body/eval_jaxpr/all_to_all | solution.py:81
  480.9 8.9 %all-to-all-start.1 = ((f32[4,2,4,512]{3,1,2,0:T(2,128)}), f32[4,2,4,512]{3,1,2,0:T(2,128)S(1)}, u32[]{:S(2)}, u32[]{:S(2)}) async-start(f32[4,2,4,512]{3,1,2,0:T(2,128)} %stack.80), calls=%async_computation.1 | async-start | bytes 131072 | tf_op jit(solution)/shard_map/while/body/eval_jaxpr/all_to_all | solution.py:81
  561.0 8.9 %all-to-all-start.1 = ((f32[4,2,4,512]{3,1,2,0:T(2,128)}), f32[4,2,4,512]{3,1,2,0:T(2,128)S(1)}, u32[]{:S(2)}, u32[]{:S(2)}) async-start(f32[4,2,4,512]{3,1,2,0:T(2,128)} %stack.80), calls=%async_computation.1 | async-start | bytes 131072 | tf_op jit(solution)/shard_map/while/body/eval_jaxpr/all_to_all | solution.py:81
  641.0 8.9 %all-to-all-start.1 = ((f32[4,2,4,512]{3,1,2,0:T(2,128)}), f32[4,2,4,512]{3,1,2,0:T(2,128)S(1)}, u32[]{:S(2)}, u32[]{:S(2)}) async-start(f32[4,2,4,512]{3,1,2,0:T(2,128)} %stack.80), calls=%async_computation.1 | async-start | bytes 131072 | tf_op jit(solution)/shard_map/while/body/eval_jaxpr/all_to_all | solution.py:81
  721.1 8.9 %all-to-all-start.1 = ((f32[4,2,4,512]{3,1,2,0:T(2,128)}), f32[4,2,4,512]{3,1,2,0:T(2,128)S(1)}, u32[]{:S(2)}, u32[]{:S(2)}) async-start(f32[4,2,4,512]{3,1,2,0:T(2,128)} %stack.80), calls=%async_computation.1 | async-start | bytes 131072 | tf_op jit(solution)/shard_map/while/body/eval_jaxpr/all_to_all | solution.py:81
  773.7 39.2 %all-to-all-start.3 = ((f32[32,1,512]{2,1,0:T(1,128)}), f32[32,1,512]{2,1,0:T(1,128)S(1)}, u32[]{:S(2)}, u32[]{:S(2)}) async-start(f32[32,1,512]{2,1,0:T(1,128)} %reshape.402), calls=%async_computation.3 | async-start | bytes 131072 | tf_op jit(solution)/shard_map/all_to_all | solution.py:101
Sparse Core Ops, SparseCore 0:
  52.2 65.9 all-gather.1
